TPU v7x, 32 devices: a whole 2x2x4 slice. The times are simulated.
32 devices in a mesh: row: 8 (over y, x, core), col: 4 (over z).
Axes of the slice: x: 2, y: 2, z: 4, core: 2. Of those that a mesh axis runs over, the one named last changes fastest.
Arguments:
- queries: bfloat16 [512, 2, 2048], P('row', None, 'col'), may hold values from -15 to 15
- new_keys: bfloat16 [512, 2, 2048], P('row', None, 'col'), may hold values from -6 to 6
- new_values: bfloat16 [512, 2, 2048], P('row', None, 'col'), may hold values from -6 to 6
- cache_keys: bfloat16 [1024, 2, 2048], P('row', None, 'col'), may hold values from -6 to 6
- cache_values: bfloat16 [1024, 2, 2048], P('row', None, 'col'), may hold values from -6 to 6
- cached_len: int32 [2], replicated, may hold values from 256 to 1024, as said below
- residual: bfloat16 [512, 2, 2048], P('row'), may hold values from -4 to 4
- out_weight: bfloat16 [2048, 2048], P('col'), may hold values from -0.125 to 0.125
- norm_gain: float32 [2048], replicated, may hold values from 0.5 to 1.5
- expert_ids: int32 [512, 2, 6], P('row'), may hold values from 0 to 63, all different within a row; in each aligned block of 128 rows (0 to 127, 128 to 255, ..., all dimensions but the last counted through in order) at most 24 rows name the same one
- gate_values: float32 [512, 2, 6], P('row'), may hold values from 0.1 to 0.6
- w_gate: bfloat16 [256, 2048, 352], P(('row', 'col')), may hold values from -0.125 to 0.125
- w_up: bfloat16 [256, 2048, 352], P(('row', 'col')), may hold values from -0.125 to 0.125
- w_down: bfloat16 [256, 352, 2048], P(('row', 'col')), may hold values from -0.15625 to 0.15625
- shared_gate: bfloat16 [2048, 2816], P(None, 'col'), may hold values from -0.125 to 0.125
- shared_up: bfloat16 [2048, 2816], P(None, 'col'), may hold values from -0.125 to 0.125
- shared_down: bfloat16 [2816, 2048], P('col'), may hold values from -0.109375 to 0.109375
Outputs:
- mixed: bfloat16 [512, 2, 2048], P('row', None, 'col')
- ffn_out: bfloat16 [512, 2, 2048], P('row', None, 'col')
Inputs may be any that keep to these rules, and one draw needn't show every extreme that they name: `cached_len`: some request has exactly 1024 cached positions. `expert_ids`: each token names 6 different experts. Among the 128 tokens of one index of row (positions taken in order, requests inside), no expert is named more than 24 times, and in some such blocks one expert is named exactly 24 times.
All inputs are finite; a program needn't handle non-finite values.
Results may differ from a plain program's by a relative error of at most 0.023.
Values may be sent and summed in bfloat16 or wider, within the bound.
No kernel may reach another device: no remote copies, remote signals or barrier semaphores. Data moves between devices by JAX's collectives and lax.ppermute only.
A program may use at most 192 MiB of HBM per device.

v0:
```python
import math
import jax
import jax.numpy as jnp
from jax import lax
from jax.sharding import PartitionSpec as P

HD = 128
E = 64
TOPK = 6
GROUPS = 4
CAP = 24


def body(
    queries,
    new_keys,
    new_values,
    cache_keys,
    cache_values,
    cached_len,
    residual,
    out_weight,
    norm_gain,
    expert_ids,
    gate_values,
    w_gate,
    w_up,
    w_down,
    shared_gate,
    shared_up,
    shared_down,
):
    rows_here = queries.shape[0]
    requests = queries.shape[1]
    heads_here = queries.shape[2] // HD
    cache_rows = cache_keys.shape[0]
    block_rows = cache_rows + rows_here
    model_width = residual.shape[2]
    row_index = lax.axis_index("row")
    row_count = lax.axis_size("row")
    score_scale = 1.0 / math.sqrt(HD)
    keys_here = jnp.concatenate([cache_keys, new_keys], axis=0)
    values_here = jnp.concatenate([cache_values, new_values], axis=0)
    query_heads = queries.reshape(rows_here, requests, heads_here, HD)
    local_pos = row_index * rows_here + jnp.arange(rows_here, dtype=jnp.int32)
    key_piece = lax.all_gather(keys_here, "row", axis=0, tiled=True)
    key_count = key_piece.shape[0]
    global_row = jnp.arange(key_count, dtype=jnp.int32)
    shard_index = global_row // block_rows
    offset_rows = global_row % block_rows
    in_cache = offset_rows < cache_rows
    cache_pos = shard_index * cache_rows + offset_rows
    new_pos = shard_index * rows_here + offset_rows - cache_rows
    cache_ok = in_cache[None, :] & (cache_pos[None, :] < cached_len[:, None])
    new_ok = jnp.logical_not(in_cache)[None, :] & (new_pos[None, :] <= local_pos[:, None])
    allowed = cache_ok[:, None, None, :] | new_ok[None, None, :, :]
    key_heads = key_piece.reshape(key_count, requests, heads_here, HD)
    value_heads = lax.all_gather(values_here, "row", axis=0, tiled=True).reshape(
        key_count, requests, heads_here, HD
    )
    scores = (
        jnp.einsum("irhd,jrhd->rhij", query_heads, key_heads, preferred_element_type=jnp.float32)
        * score_scale
    )
    masked = jnp.where(allowed, scores, -1e30)
    old_max = jnp.full((requests, heads_here, rows_here), -1e30, jnp.float32)
    new_max = jnp.maximum(old_max, jnp.max(masked, axis=-1))
    weights_now = jnp.where(allowed, jnp.exp(masked - new_max[..., None]), 0.0)
    new_sum = jnp.sum(weights_now, axis=-1)
    product = jnp.einsum(
        "rhij,jrhd->rhid",
        weights_now.astype(jnp.bfloat16),
        value_heads,
        preferred_element_type=jnp.float32,
    )
    attended = (product / new_sum[..., None]).astype(jnp.bfloat16)
    head_weights = out_weight.reshape(heads_here, HD, model_width)
    attn_part = jnp.einsum(
        "rhid,hde->ire", attended, head_weights, preferred_element_type=jnp.float32
    )
    attn_full = lax.psum(attn_part.astype(jnp.bfloat16), "col").astype(jnp.float32)
    mixed_full = (residual.astype(jnp.float32) + attn_full).astype(jnp.bfloat16)
    mixed_f32 = mixed_full.astype(jnp.float32)
    normed = (
        mixed_f32
        * lax.rsqrt(jnp.mean(mixed_f32 * mixed_f32, axis=-1, keepdims=True) + 1e-06)
        * norm_gain
    ).astype(jnp.bfloat16)
    token_count = rows_here * requests
    tokens = normed.reshape(token_count, model_width)
    col_index = lax.axis_index("col")
    col_count = lax.axis_size("col")
    entries_here = w_gate.shape[0]
    experts_dev = max(1, entries_here // GROUPS)
    groups_dev = entries_here // experts_dev
    experts_per_row = col_count * entries_here // GROUPS
    slots = row_count * experts_dev * CAP
    chosen = expert_ids.reshape(token_count * TOPK)
    onehot = (chosen[:, None] == jnp.arange(E, dtype=jnp.int32)[None, :]).astype(jnp.int32)
    slot_index = jnp.sum(jnp.cumsum(onehot, axis=0) * onehot, axis=1) - 1
    dest_row = chosen // experts_per_row
    local_expert = chosen - (dest_row * col_count + col_index) * entries_here // GROUPS
    valid = (local_expert >= 0) & (local_expert < experts_dev)
    place = (dest_row * experts_dev + local_expert) * CAP + slot_index
    place = jnp.where(valid, place, -1).reshape(token_count, TOPK)
    hit = place[:, :, None] == jnp.arange(slots, dtype=jnp.int32)[None, None, :]
    dispatch = jnp.sum(hit.astype(jnp.float32), axis=1).astype(jnp.bfloat16)
    combine = jnp.sum(jnp.where(hit, gate_values.reshape(token_count, TOPK, 1), 0.0), axis=1)
    outgoing = lax.dot_general(
        dispatch, tokens, (((0,), (0,)), ((), ())), preferred_element_type=jnp.float32
    ).astype(jnp.bfloat16)
    outgoing = outgoing.reshape(row_count, experts_dev, CAP, model_width)
    arrived = lax.all_to_all(outgoing, "row", 0, 0, tiled=True)
    hidden = w_gate.shape[2]
    wg = w_gate.reshape(experts_dev, groups_dev, model_width, hidden)
    wu = w_up.reshape(experts_dev, groups_dev, model_width, hidden)
    wd = w_down.reshape(experts_dev, groups_dev, hidden, model_width)
    gate_proj = jnp.einsum("nlsd,lgdf->lgnsf", arrived, wg, preferred_element_type=jnp.float32)
    up_proj = jnp.einsum("nlsd,lgdf->lgnsf", arrived, wu, preferred_element_type=jnp.float32)
    hidden_act = (jax.nn.silu(gate_proj) * up_proj).astype(jnp.bfloat16)
    expert_out = jnp.einsum(
        "lgnsf,lgfd->nlsd", hidden_act, wd, preferred_element_type=jnp.float32
    ).astype(jnp.bfloat16)
    returned = lax.all_to_all(expert_out, "row", 0, 0, tiled=True).reshape(slots, model_width)
    combine_hi = combine.astype(jnp.bfloat16)
    combine_lo = (combine - combine_hi.astype(jnp.float32)).astype(jnp.bfloat16)
    routed = jnp.dot(combine_hi, returned, preferred_element_type=jnp.float32) + jnp.dot(
        combine_lo, returned, preferred_element_type=jnp.float32
    )
    shared_g = jnp.dot(tokens, shared_gate, preferred_element_type=jnp.float32)
    shared_u = jnp.dot(tokens, shared_up, preferred_element_type=jnp.float32)
    shared_act = (jax.nn.silu(shared_g) * shared_u).astype(jnp.bfloat16)
    shared_part = jnp.dot(shared_act, shared_down, preferred_element_type=jnp.float32)
    ffn_total = lax.psum_scatter(
        (routed + shared_part).astype(jnp.bfloat16), "col", scatter_dimension=1, tiled=True
    )
    col_width = model_width // col_count
    ffn_here = ffn_total.reshape(rows_here, requests, col_width)
    mixed_here = lax.dynamic_slice_in_dim(mixed_full, col_index * col_width, col_width, 2)
    return (mixed_here, ffn_here)


def solution(mesh):
    in_specs = (
        P("row", None, "col"),
        P("row", None, "col"),
        P("row", None, "col"),
        P("row", None, "col"),
        P("row", None, "col"),
        P(),
        P("row", None, None),
        P("col", None),
        P(),
        P("row", None, None),
        P("row", None, None),
        P(("row", "col"), None, None),
        P(("row", "col"), None, None),
        P(("row", "col"), None, None),
        P(None, "col"),
        P(None, "col"),
        P("col", None),
    )
    out_specs = (P("row", None, "col"), P("row", None, "col"))
    return jax.shard_map(body, mesh=mesh, in_specs=in_specs, out_specs=out_specs, check_vma=False)
```

profile of v0, /device:TPU:0, one launch (start us, length us, event | category | flops | bytes accessed | tf_op | source)
XLA Modules:
  0.0 250.1 jit_solution(14127599166133961431)
XLA Ops:
  7.2 2.4 pad_maximum_fusion
  9.8 2.3 pad_maximum_fusion.1
  12.1 0.8 copy.73
  13.2 1.0 reshape.257
  14.2 1.8 reduce-window.6
  16.9 28.1 %all-gather.3.cloned.1.call-done = bf16[1536,2,512]{2,1,0:T(2,128)(2,1)} async-done(((bf16[192,2,512]{2,1,0:T(2,128)(2,1)}), bf16[1536,2,512]{2,1,0:T(2,128)(2,1)}) %all-gather.3.cloned.1.call-update) | async-done | bytes 3145744 | tf_op jit(solution)/shard_map/all_gather | solution.py:46
  45.0 8.7 %copy.68 = bf16[1536,2,512]{0,2,1:T(8,128)(2,1)} copy(bf16[1536,2,512]{2,1,0:T(2,128)(2,1)} %all-gather.3.cloned.1.call-done) | data formatting | bytes 6291456 | tf_op jit(solution)/shard_map/all_gather | solution.py:46
  53.7 3.0 %fusion.62 = (f32[2,4,64]{2,1,0:T(4,128)S(1)}, f32[2,4,64,1536]{3,2,1,0:T(8,128)S(1)}) fusion(bf16[1536,2,4,128]{0,3,2,1:T(8,128)(2,1)} %bitcast.114, bf16[64,2,4,128]{3,2,1,0:T(4,128)(2,1)S(1)} %reshape.257, pred[2,64,1536]{2,1,0:T(8,128)(4,1)S(1)} %broadcast_or_fusion), kind=kOutput, calls=%fused_computation.106 | convolution fusion | flops 203685376 | bytes 6621184 | tf_op jit(solution)/shard_map/irhd,jrhd->rhij/dot_general | solution.py:62
  56.7 1.7 copy-done.1
  58.4 0.8 fusion.3
  59.2 20.0 %all-gather.5.cloned.1.call-done = bf16[1536,2,512]{2,1,0:T(2,128)(2,1)} async-done(((bf16[192,2,512]{2,1,0:T(2,128)(2,1)}), bf16[1536,2,512]{2,1,0:T(2,128)(2,1)}) %all-gather.5.cloned.1.call-update) | async-done | bytes 3145744 | tf_op jit(solution)/shard_map/all_gather | solution.py:58
  79.2 8.7 %copy.71 = bf16[1536,2,512]{0,2,1:T(8,128)(2,1)} copy(bf16[1536,2,512]{2,1,0:T(2,128)(2,1)} %all-gather.5.cloned.1.call-done) | data formatting | bytes 6291456 | tf_op jit(solution)/shard_map/all_gather | solution.py:58
  87.9 5.9 %fusion.11 = bf16[64,2,2048]{2,0,1:T(8,128)(2,1)} fusion(bf16[4,128,2048,1]{2,1,0,3:T(8,128)(2,1)} %bitcast.123, bf16[1536,2,4,128]{0,3,2,1:T(8,128)(2,1)} %bitcast.116, f32[2,4,64,1536]{3,2,1,0:T(8,128)} %copy-done.1, f32[2,4,64]{2,1,0:T(4,128)S(1)} %broadcast_maximum_fusion, pred[2,64,1536]{2,1,0:T(8,128)(4,1)S(1)} %broadcast_or_fusion, ...), kind=kOutput, calls=%fused_computation.21 | convolution fusion | flops 472514560 | bytes 9113600 | tf_op jit(solution)/shard_map/rhid,hde->ire/dot_general | solution.py:78
  94.3 1.0 select_reduce_fusion
  95.3 37.0 %all-reduce.2.cloned.1.call-done = bf16[64,2,2048]{2,0,1:T(8,128)(2,1)} async-done(((bf16[64,2,2048]{2,0,1:T(8,128)(2,1)}), bf16[64,2,2048]{2,0,1:T(8,128)(2,1)}) %all-reduce.2.cloned.1.call-update) | async-done | bytes 524304 | tf_op jit(solution)/shard_map/psum | solution.py:81
  132.3 1.5 fusion.29
  133.8 0.8 copy-done.2
  134.8 1.3 copy.80
  136.2 1.2 reshape.262
  138.0 24.4 %all_to_all.10 = bf16[8,2,24,2048]{3,2,1,0:T(8,128)(2,1)S(1)} all-to-all(bf16[8,2,24,2048]{3,2,1,0:T(8,128)(2,1)S(1)} %bitcast.115), channel_id=1, replica_groups=mesh['row'=8,'col'=4] {'row'}, dimensions={0} | all-to-all | bytes 3145728 | tf_op jit(solution)/shard_map/all_to_all | solution.py:113
  162.4 8.5 %fusion.17 = f32[2,8,24,4,352]{4,2,3,1,0:T(8,128)} fusion(bf16[2,4,2048,352,1]{2,3,1,4,0:T(8,128)(2,1)} %bitcast.120, bf16[8,2,24,2048]{3,2,1,0:T(8,128)(2,1)S(1)} %all_to_all.10), kind=kOutput, calls=%fused_computation.26 | convolution fusion | flops 2214592512 | bytes 15269888 | tf_op jit(solution)/shard_map/nlsd,lgdf->lgnsf/dot_general | solution.py:119
  171.0 12.9 %fusion.2 = bf16[8,2,24,2048]{3,2,0,1:T(8,128)(2,1)} fusion(bf16[2,4,352,2048,1]{3,2,1,4,0:T(8,128)(2,1)} %bitcast.121, f32[2,8,24,4,352]{4,2,3,1,0:T(8,128)} %fusion.17, bf16[2,4,2048,352,1]{2,3,1,4,0:T(8,128)(2,1)} %bitcast.122, bf16[8,2,24,2048]{3,2,1,0:T(8,128)(2,1)} %copy-done.4), kind=kOutput, calls=%fused_computation.6 | convolution fusion | flops 4433215488 | bytes 28377088 | tf_op jit(solution)/shard_map/lgnsf,lgfd->nlsd/dot_general | solution.py:121
  183.9 2.7 %copy.83 = bf16[8,2,24,2048]{3,2,1,0:T(8,128)(2,1)} copy(bf16[8,2,24,2048]{3,2,0,1:T(8,128)(2,1)} %fusion.2) | data formatting | bytes 3145728 | tf_op jit(solution)/shard_map/convert_element_type | solution.py:123
  186.6 4.3 %all-to-all-start.1 = ((bf16[8,2,24,2048]{3,2,1,0:T(8,128)(2,1)}), bf16[8,2,24,2048]{3,2,1,0:T(8,128)(2,1)}, u32[]{:S(2)}, u32[]{:S(2)}) async-start(bf16[8,2,24,2048]{3,2,1,0:T(8,128)(2,1)} %copy.83), calls=%async_computation.1 | async-start | bytes 3145728 | tf_op jit(solution)/shard_map/all_to_all | solution.py:124
  191.0 3.5 %fusion.63 = f32[128,704]{0,1:T(8,128)} fusion(bf16[128,2048]{1,0:T(8,128)(2,1)S(1)} %reshape.262, bf16[2048,704]{0,1:T(8,128)(2,1)} %param.31), kind=kOutput, calls=%fused_computation.107 | convolution fusion | flops 369098752 | bytes 3768320 | tf_op jit(solution)/shard_map/dot_general | solution.py:130
  194.4 17.5 %all-to-all-done.1 = bf16[8,2,24,2048]{3,2,1,0:T(8,128)(2,1)} async-done(((bf16[8,2,24,2048]{3,2,1,0:T(8,128)(2,1)}), bf16[8,2,24,2048]{3,2,1,0:T(8,128)(2,1)}, u32[]{:S(2)}, u32[]{:S(2)}) %all-to-all-start.1) | async-done | bytes 1572896 | tf_op jit(solution)/shard_map/all_to_all | solution.py:124
  212.0 2.0 fusion.50
  214.0 2.8 %convolution_add_fusion.1 = f32[128,2048]{1,0:T(8,128)} fusion(f32[128,2048]{1,0:T(8,128)S(1)} %fusion.50, bf16[384,2048]{1,0:T(8,128)(2,1)} %bitcast.28, f32[128,384]{1,0:T(8,128)S(1)} %copy-done.3), kind=kOutput, calls=%fused_computation.10 | convolution fusion | flops 201785344 | bytes 3866624 | tf_op jit(solution)/shard_map/dot_general | solution.py:127
  216.8 5.1 %fusion.5 = bf16[128,2048]{1,0:T(8,128)(2,1)} fusion(f32[128,2048]{1,0:T(8,128)} %convolution_add_fusion.1, bf16[704,2048]{1,0:T(8,128)(2,1)S(1)} %copy-done, bf16[128,2048]{1,0:T(8,128)(2,1)S(1)} %reshape.262, bf16[2048,704]{0,1:T(8,128)(2,1)} %param.32, f32[128,704]{0,1:T(8,128)} %fusion.63), kind=kOutput, calls=%fused_computation.12 | convolution fusion | flops 739262464 | bytes 8224768 | tf_op jit(solution)/shard_map/dot_general | solution.py:133
  221.9 0.9 constant_dynamic-slice_fusion
  223.7 18.3 %reduce-scatter.2.cloned.1.call-done = bf16[128,512]{1,0:T(8,128)(2,1)} async-done(((bf16[128,2048]{1,0:T(8,128)(2,1)}), bf16[128,512]{1,0:T(8,128)(2,1)}) %reduce-scatter.2.cloned.1.call-update) | async-done | bytes 131088 | tf_op jit(solution)/shard_map/reduce_scatter | solution.py:134
  241.9 1.6 reshape.268
  (47 shorter events, 3.4 us)
Async XLA Ops:
  7.2 209.6 %copy-start = (bf16[704,2048]{1,0:T(8,128)(2,1)S(1)}, bf16[704,2048]{1,0:T(8,128)(2,1)}, u32[]{:S(2)}) copy-start(bf16[704,2048]{1,0:T(8,128)(2,1)} %param.33) | copy-start | bytes 8650756
  7.2 9.4 %copy-start.7 = (s32[2]{0:T(128)S(1)}, s32[2]{0:T(128)}, u32[]{:S(2)}) copy-start(s32[2]{0:T(128)} %param.22) | copy-start | bytes 28
  7.2 37.8 %all-gather.3.cloned.1.call-start = ((), (), s32[]{:S(2)}) async-start(), calls=%async_computation.3 | async-start | bytes 3538944 | tf_op jit(solution)/shard_map/all_gather | solution.py:46
  9.7 69.5 %all-gather.5.cloned.1.call-start = ((), (), s32[]{:S(2)}) async-start(), calls=%async_computation.4 | async-start | bytes 3538944 | tf_op jit(solution)/shard_map/all_gather | solution.py:58
  12.1 120.3 %all-reduce.2.cloned.1.call-start = ((), (), s32[]{:S(2)}) async-start(), calls=%async_computation.5 | async-start | bytes 1048576 | tf_op jit(solution)/shard_map/psum | solution.py:81
  56.7 1.7 copy-start.1
  87.9 6.3 %copy-start.6 = (f32[64,2,6]{0,1,2:T(2,128)S(1)}, f32[64,2,6]{0,1,2:T(2,128)}, u32[]{:S(2)}) copy-start(f32[64,2,6]{0,1,2:T(2,128)} %param.27) | copy-start | bytes 9220
  93.8 40.9 %copy-start.5 = (f32[2048]{0:T(1024)S(1)}, f32[2048]{0:T(1024)}, u32[]{:S(2)}) copy-start(f32[2048]{0:T(1024)} %param.25) | copy-start | bytes 24580
  133.8 0.8 copy-start.2
  162.4 8.5 %copy-start.4 = (bf16[8,2,24,2048]{3,2,1,0:T(8,128)(2,1)}, bf16[8,2,24,2048]{3,2,1,0:T(8,128)(2,1)S(1)}, u32[]{:S(2)}) copy-start(bf16[8,2,24,2048]{3,2,1,0:T(8,128)(2,1)S(1)} %all_to_all.10) | copy-start | bytes 4718596
  186.6 25.3 %all-to-all-start.1 = ((bf16[8,2,24,2048]{3,2,1,0:T(8,128)(2,1)}), bf16[8,2,24,2048]{3,2,1,0:T(8,128)(2,1)}, u32[]{:S(2)}, u32[]{:S(2)}) async-start(bf16[8,2,24,2048]{3,2,1,0:T(8,128)(2,1)} %copy.83), calls=%async_computation.1 | async-start | bytes 3145728 | tf_op jit(solution)/shard_map/all_to_all | solution.py:124
  190.9 51.0 %reduce-scatter.2.cloned.1.call-start = ((), (), s32[]{:S(2)}) async-start(), calls=%async_computation.6 | async-start | bytes 655360 | tf_op jit(solution)/shard_map/reduce_scatter | solution.py:134
  212.0 2.0 copy-start.3
Sparse Core Ops, SparseCore 0:
  9.9 35.0 all-gather.2
  46.8 32.3 all-gather.4
  93.9 38.3 all-reduce.1
  222.1 19.8 reduce-scatter.1
where the time goes:
time: 251 us; the launch traced here: 250 us
  waiting for transfers between devices  121 us (48%)
  matrix products  44.3 us (18%)
  local copies, waits for them, and re-layouts  31.3 us (12%)
  blocking collectives  24.4 us (10%)
  between operations  14 us (6%)
  other arithmetic  10.7 us (4%)
  starting transfers between devices  4.45 us (2%)
    psum x1, waiting for transfers between devices, body(): lax.psum(attn_part.astype(jnp.bfloat16), 'col').astype(jnp.float32)  37 us
    all_gather x1, waiting for transfers between devices, body(): key_piece = lax.all_gather(keys_here, 'row', axis=0, tiled=True)  28.1 us
    all_to_all x1, blocking collectives, body(): arrived = lax.all_to_all(outgoing, 'row', 0, 0, tiled=True)  24.4 us
    all_gather x1, waiting for transfers between devices, body(): lax.all_gather(values_here, 'row', axis=0, tiled=True)  20 us
    reduce_scatter x1, waiting for transfers between devices, body(): lax.psum_scatter((routed + shared_part).astype(jnp.bfloat16), 'col', scat...  18.3 us
    all_to_all x1, waiting for transfers between devices, body(): lax.all_to_all(expert_out, 'row', 0, 0, tiled=True)  17.5 us
    dot_general x1, matrix products, body(): jnp.einsum('lgnsf,lgfd->nlsd', hidden_act, wd, preferred_element_type=jnp...  12.9 us
    all_gather x1, local copies, waits for them, and re-layouts, body(): key_piece = lax.all_gather(keys_here, 'row', axis=0, tiled=True)  8.71 us
  transfers between devices with their start and end apart: 5, of which 5 were waited for; matrix products, arithmetic and copies ran while one was open for 10% of the time, Pallas kernels for 0%

commit v1 on v0

--- a/solution.py
+++ b/solution.py
@@ -9,6 +9,11 @@
 TOPK = 6
 GROUPS = 4
 CAP = 24
+
+
+def update_quarters(sample):
+    low = jnp.sum(lax.all_gather(sample, "col"), 0)
+    return low
 
 
 def body(
@@ -78,7 +83,7 @@
     attn_part = jnp.einsum(
         "rhid,hde->ire", attended, head_weights, preferred_element_type=jnp.float32
     )
-    attn_full = lax.psum(attn_part.astype(jnp.bfloat16), "col").astype(jnp.float32)
+    attn_full = update_quarters(attn_part.astype(jnp.bfloat16)).astype(jnp.float32)
     mixed_full = (residual.astype(jnp.float32) + attn_full).astype(jnp.bfloat16)
     mixed_f32 = mixed_full.astype(jnp.float32)
     normed = (

time: 251 us -> 259 us (1.032)
  waiting for transfers between devices: 121 us -> 127 us
    all_gather x0 -> x1, waiting for transfers between devices: none -> 41.9 us  [update_quarters(): low = jnp.sum(lax.all_gather(sample, 'col'), 0)]
    psum x1 -> x0, waiting for transfers between devices: 37 us -> none  [body(): lax.psum(attn_part.astype(jnp.bfloat16), 'col').astype(jnp.float32)]
    all_gather x1, waiting for transfers between devices: 28.1 us -> 30.8 us  [body(): key_piece = lax.all_gather(keys_here, 'row', axis=0, tiled=True)]
where the time goes in v1:
time: 259 us; the launch traced here: 258 us
  waiting for transfers between devices  127 us (49%)
  matrix products  44.3 us (17%)
  local copies, waits for them, and re-layouts  30.7 us (12%)
  blocking collectives  24.4 us (9%)
  between operations  14 us (5%)
  other arithmetic  13.2 us (5%)
  starting transfers between devices  4.45 us (2%)
    all_gather x1, waiting for transfers between devices, update_quarters(): low = jnp.sum(lax.all_gather(sample, 'col'), 0)  41.9 us
    all_gather x1, waiting for transfers between devices, body(): key_piece = lax.all_gather(keys_here, 'row', axis=0, tiled=True)  30.8 us
    all_to_all x1, blocking collectives, body(): arrived = lax.all_to_all(outgoing, 'row', 0, 0, tiled=True)  24.4 us
    all_gather x1, waiting for transfers between devices, body(): lax.all_gather(values_here, 'row', axis=0, tiled=True)  20 us
    all_to_all x1, waiting for transfers between devices, body(): lax.all_to_all(expert_out, 'row', 0, 0, tiled=True)  17.5 us
    reduce_scatter x1, waiting for transfers between devices, body(): lax.psum_scatter((routed + shared_part).astype(jnp.bfloat16), 'col', scat...  17 us
    dot_general x1, matrix products, body(): jnp.einsum('lgnsf,lgfd->nlsd', hidden_act, wd, preferred_element_type=jnp...  12.9 us
    all_gather x1, local copies, waits for them, and re-layouts, body(): key_piece = lax.all_gather(keys_here, 'row', axis=0, tiled=True)  8.71 us
  transfers between devices with their start and end apart: 5, of which 5 were waited for; matrix products, arithmetic and copies ran while one was open for 10% of the time, Pallas kernels for 0%

profile of v1, /device:TPU:0, one launch (start us, length us, event | category | flops | bytes accessed | tf_op | source)
XLA Modules:
  0.0 258.3 jit_solution(4001844207295902741)
XLA Ops:
  7.2 2.4 pad_maximum_fusion
  9.7 2.3 pad_maximum_fusion.1
  12.1 1.0 reshape.257
  14.2 30.8 %all-gather.5.cloned.1.call-done = bf16[1536,2,512]{2,1,0:T(2,128)(2,1)} async-done(((bf16[192,2,512]{2,1,0:T(2,128)(2,1)}), bf16[1536,2,512]{2,1,0:T(2,128)(2,1)}) %all-gather.5.cloned.1.call-update) | async-done | bytes 3145744 | tf_op jit(solution)/shard_map/all_gather | solution.py:51
  44.9 8.7 %copy.62 = bf16[1536,2,512]{0,2,1:T(8,128)(2,1)} copy(bf16[1536,2,512]{2,1,0:T(2,128)(2,1)} %all-gather.5.cloned.1.call-done) | data formatting | bytes 6291456 | tf_op jit(solution)/shard_map/all_gather | solution.py:51
  53.7 3.0 %fusion.62 = (f32[2,4,64]{2,1,0:T(4,128)S(1)}, f32[2,4,64,1536]{3,2,1,0:T(8,128)S(1)}) fusion(bf16[1536,2,4,128]{0,3,2,1:T(8,128)(2,1)} %bitcast.115, bf16[64,2,4,128]{3,2,1,0:T(4,128)(2,1)S(1)} %reshape.257, pred[2,64,1536]{2,1,0:T(8,128)(4,1)S(1)} %broadcast_or_fusion), kind=kOutput, calls=%fused_computation.106 | convolution fusion | flops 203685376 | bytes 6621184 | tf_op jit(solution)/shard_map/irhd,jrhd->rhij/dot_general | solution.py:67
  56.7 1.7 copy-done.1
  58.4 0.8 fusion.3
  59.2 20.0 %all-gather.7.cloned.1.call-done = bf16[1536,2,512]{2,1,0:T(2,128)(2,1)} async-done(((bf16[192,2,512]{2,1,0:T(2,128)(2,1)}), bf16[1536,2,512]{2,1,0:T(2,128)(2,1)}) %all-gather.7.cloned.1.call-update) | async-done | bytes 3145744 | tf_op jit(solution)/shard_map/all_gather | solution.py:63
  79.2 8.7 %copy.65 = bf16[1536,2,512]{0,2,1:T(8,128)(2,1)} copy(bf16[1536,2,512]{2,1,0:T(2,128)(2,1)} %all-gather.7.cloned.1.call-done) | data formatting | bytes 6291456 | tf_op jit(solution)/shard_map/all_gather | solution.py:63
  87.9 5.9 %fusion.11 = bf16[64,2,2048]{2,0,1:T(8,128)(2,1)} fusion(bf16[4,128,2048,1]{2,1,0,3:T(8,128)(2,1)} %bitcast.125, bf16[1536,2,4,128]{0,3,2,1:T(8,128)(2,1)} %bitcast.117, f32[2,4,64,1536]{3,2,1,0:T(8,128)} %copy-done.1, f32[2,4,64]{2,1,0:T(4,128)S(1)} %broadcast_maximum_fusion, pred[2,64,1536]{2,1,0:T(8,128)(4,1)S(1)} %broadcast_or_fusion, ...), kind=kOutput, calls=%fused_computation.21 | convolution fusion | flops 472514560 | bytes 9113600 | tf_op jit(solution)/shard_map/rhid,hde->ire/dot_general | solution.py:83
  94.3 1.8 reduce-window.6
  97.1 1.0 select_reduce_fusion
  98.1 41.9 %all-gather.9.cloned.1.call-done = bf16[256,2,2048]{2,0,1:T(8,128)(2,1)} async-done(((bf16[64,2,2048]{2,0,1:T(8,128)(2,1)}), bf16[256,2,2048]{2,0,1:T(8,128)(2,1)}) %all-gather.9.cloned.1.call-update) | async-done | bytes 2097168 | tf_op jit(solution)/shard_map/all_gather | solution.py:15
  140.0 2.0 reduce_sum.58
  142.0 1.3 fusion.29
  143.4 0.8 copy-done.2
  144.4 1.3 copy.74
  145.7 1.2 reshape.262
  147.5 24.4 %all_to_all.10 = bf16[8,2,24,2048]{3,2,1,0:T(8,128)(2,1)S(1)} all-to-all(bf16[8,2,24,2048]{3,2,1,0:T(8,128)(2,1)S(1)} %bitcast.116), channel_id=1, replica_groups=mesh['row'=8,'col'=4] {'row'}, dimensions={0} | all-to-all | bytes 3145728 | tf_op jit(solution)/shard_map/all_to_all | solution.py:118
  172.0 8.5 %fusion.17 = f32[2,8,24,4,352]{4,2,3,1,0:T(8,128)} fusion(bf16[2,4,2048,352,1]{2,3,1,4,0:T(8,128)(2,1)} %bitcast.122, bf16[8,2,24,2048]{3,2,1,0:T(8,128)(2,1)S(1)} %all_to_all.10), kind=kOutput, calls=%fused_computation.26 | convolution fusion | flops 2214592512 | bytes 15269888 | tf_op jit(solution)/shard_map/nlsd,lgdf->lgnsf/dot_general | solution.py:124
  180.5 12.9 %fusion.2 = bf16[8,2,24,2048]{3,2,0,1:T(8,128)(2,1)} fusion(bf16[2,4,352,2048,1]{3,2,1,4,0:T(8,128)(2,1)} %bitcast.123, f32[2,8,24,4,352]{4,2,3,1,0:T(8,128)} %fusion.17, bf16[2,4,2048,352,1]{2,3,1,4,0:T(8,128)(2,1)} %bitcast.124, bf16[8,2,24,2048]{3,2,1,0:T(8,128)(2,1)} %copy-done.4), kind=kOutput, calls=%fused_computation.6 | convolution fusion | flops 4433215488 | bytes 28377088 | tf_op jit(solution)/shard_map/lgnsf,lgfd->nlsd/dot_general | solution.py:126
  193.4 2.7 %copy.77 = bf16[8,2,24,2048]{3,2,1,0:T(8,128)(2,1)} copy(bf16[8,2,24,2048]{3,2,0,1:T(8,128)(2,1)} %fusion.2) | data formatting | bytes 3145728 | tf_op jit(solution)/shard_map/convert_element_type | solution.py:128
  196.1 4.3 %all-to-all-start.1 = ((bf16[8,2,24,2048]{3,2,1,0:T(8,128)(2,1)}), bf16[8,2,24,2048]{3,2,1,0:T(8,128)(2,1)}, u32[]{:S(2)}, u32[]{:S(2)}) async-start(bf16[8,2,24,2048]{3,2,1,0:T(8,128)(2,1)} %copy.77), calls=%async_computation.1 | async-start | bytes 3145728 | tf_op jit(solution)/shard_map/all_to_all | solution.py:129
  200.5 3.5 %fusion.63 = f32[128,704]{0,1:T(8,128)} fusion(bf16[128,2048]{1,0:T(8,128)(2,1)S(1)} %reshape.262, bf16[2048,704]{0,1:T(8,128)(2,1)} %param.31), kind=kOutput, calls=%fused_computation.107 | convolution fusion | flops 369098752 | bytes 3768320 | tf_op jit(solution)/shard_map/dot_general | solution.py:135
  203.9 17.5 %all-to-all-done.1 = bf16[8,2,24,2048]{3,2,1,0:T(8,128)(2,1)} async-done(((bf16[8,2,24,2048]{3,2,1,0:T(8,128)(2,1)}), bf16[8,2,24,2048]{3,2,1,0:T(8,128)(2,1)}, u32[]{:S(2)}, u32[]{:S(2)}) %all-to-all-start.1) | async-done | bytes 1572896 | tf_op jit(solution)/shard_map/all_to_all | solution.py:129
  221.5 2.0 fusion.50
  223.5 2.8 %convolution_add_fusion.1 = f32[128,2048]{1,0:T(8,128)} fusion(f32[128,2048]{1,0:T(8,128)S(1)} %fusion.50, bf16[384,2048]{1,0:T(8,128)(2,1)} %bitcast.29, f32[128,384]{1,0:T(8,128)S(1)} %copy-done.3), kind=kOutput, calls=%fused_computation.10 | convolution fusion | flops 201785344 | bytes 3866624 | tf_op jit(solution)/shard_map/dot_general | solution.py:132
  226.3 5.1 %fusion.5 = bf16[128,2048]{1,0:T(8,128)(2,1)} fusion(f32[128,2048]{1,0:T(8,128)} %convolution_add_fusion.1, bf16[704,2048]{1,0:T(8,128)(2,1)S(1)} %copy-done, bf16[128,2048]{1,0:T(8,128)(2,1)S(1)} %reshape.262, bf16[2048,704]{0,1:T(8,128)(2,1)} %param.32, f32[128,704]{0,1:T(8,128)} %fusion.63), kind=kOutput, calls=%fused_computation.12 | convolution fusion | flops 739262464 | bytes 8224768 | tf_op jit(solution)/shard_map/dot_general | solution.py:138
  231.5 0.9 constant_dynamic-slice_fusion
  233.2 17.0 %reduce-scatter.2.cloned.1.call-done = bf16[128,512]{1,0:T(8,128)(2,1)} async-done(((bf16[128,2048]{1,0:T(8,128)(2,1)}), bf16[128,512]{1,0:T(8,128)(2,1)}) %reduce-scatter.2.cloned.1.call-update) | async-done | bytes 131088 | tf_op jit(solution)/shard_map/reduce_scatter | solution.py:139
  250.2 1.6 reshape.268
  (48 shorter events, 4.2 us)
Async XLA Ops:
  7.2 219.1 %copy-start = (bf16[704,2048]{1,0:T(8,128)(2,1)S(1)}, bf16[704,2048]{1,0:T(8,128)(2,1)}, u32[]{:S(2)}) copy-start(bf16[704,2048]{1,0:T(8,128)(2,1)} %param.33) | copy-start | bytes 8650756
  7.2 37.8 %all-gather.5.cloned.1.call-start = ((), (), s32[]{:S(2)}) async-start(), calls=%async_computation.3 | async-start | bytes 3538944 | tf_op jit(solution)/shard_map/all_gather | solution.py:51
  9.7 69.5 %all-gather.7.cloned.1.call-start = ((), (), s32[]{:S(2)}) async-start(), calls=%async_computation.4 | async-start | bytes 3538944 | tf_op jit(solution)/shard_map/all_gather | solution.py:63
  12.0 127.9 %all-gather.9.cloned.1.call-start = ((), (), s32[]{:S(2)}) async-start(), calls=%async_computation.6 | async-start | bytes 2621440 | tf_op jit(solution)/shard_map/all_gather | solution.py:15
  56.7 1.7 copy-start.1
  87.9 5.9 %copy-start.6 = (s32[64,2,6]{0,1,2:T(2,128)S(1)}, s32[64,2,6]{0,1,2:T(2,128)}, u32[]{:S(2)}) copy-start(s32[64,2,6]{0,1,2:T(2,128)} %param.26) | copy-start | bytes 9220
  87.9 9.0 %copy-start.7 = (f32[64,2,6]{0,1,2:T(2,128)S(1)}, f32[64,2,6]{0,1,2:T(2,128)}, u32[]{:S(2)}) copy-start(f32[64,2,6]{0,1,2:T(2,128)} %param.27) | copy-start | bytes 9220
  94.3 49.9 %copy-start.5 = (f32[2048]{0:T(1024)S(1)}, f32[2048]{0:T(1024)}, u32[]{:S(2)}) copy-start(f32[2048]{0:T(1024)} %param.25) | copy-start | bytes 24580
  143.3 0.8 copy-start.2
  172.0 8.5 %copy-start.4 = (bf16[8,2,24,2048]{3,2,1,0:T(8,128)(2,1)}, bf16[8,2,24,2048]{3,2,1,0:T(8,128)(2,1)S(1)}, u32[]{:S(2)}) copy-start(bf16[8,2,24,2048]{3,2,1,0:T(8,128)(2,1)S(1)} %all_to_all.10) | copy-start | bytes 4718596
  196.1 25.3 %all-to-all-start.1 = ((bf16[8,2,24,2048]{3,2,1,0:T(8,128)(2,1)}), bf16[8,2,24,2048]{3,2,1,0:T(8,128)(2,1)}, u32[]{:S(2)}, u32[]{:S(2)}) async-start(bf16[8,2,24,2048]{3,2,1,0:T(8,128)(2,1)} %copy.77), calls=%async_computation.1 | async-start | bytes 3145728 | tf_op jit(solution)/shard_map/all_to_all | solution.py:129
  200.4 49.8 %reduce-scatter.2.cloned.1.call-start = ((), (), s32[]{:S(2)}) async-start(), calls=%async_computation.5 | async-start | bytes 655360 | tf_op jit(solution)/shard_map/reduce_scatter | solution.py:139
  221.5 2.0 copy-start.3
Sparse Core Ops, SparseCore 0:
  9.9 35.0 all-gather.4
  46.8 32.3 all-gather.6
  94.0 45.9 all-gather.8
  231.6 18.5 reduce-scatter.1
